TPU v7x, 32 devices: a whole 2x2x4 slice. The times are simulated.
32 devices in a mesh: seq: 8 (over z, y), exp: 4 (over x, core).
Axes of the slice: x: 2, y: 2, z: 4, core: 2. Of those that a mesh axis runs over, the one named last changes fastest.
Arguments:
- hidden: bfloat16 [4, 1024, 2048], P('exp', 'seq'), may hold values from -6 to 6
- lengths: int32 [4, 4], P('exp'), may hold values from 1 to 512, 1024 in all within a row
- attn_gain: float32 [2048], replicated, may hold values from 0 to 10
- w_qkv: bfloat16 [2048, 3, 16, 128], P(None, None, 'seq'), may hold values from -0.125 to 0.125
- w_out: bfloat16 [16, 128, 2048], P('seq'), may hold values from -0.125 to 0.125
- moe_gain: float32 [2048], replicated, may hold values from 0.5 to 1.5
- router: bfloat16 [2048, 16], replicated, may hold values from -8 to 8
- routes: int32 [4, 1024, 6], P('exp', 'seq'), may hold values from 0 to 15, all different within a row; in each aligned block of 128 rows (0 to 127, 128 to 255, ..., all dimensions but the last counted through in order) at most 56 rows name the same one
- w_gate_up: bfloat16 [32, 2, 704, 2048], P(('seq', 'exp')), may hold values from -0.125 to 0.125
- w_down: bfloat16 [32, 704, 2048], P(('seq', 'exp')), may hold values from -0.15625 to 0.15625
- final_gain: float32 [2048], replicated, may hold values from 0.5 to 1.5
- lm_head: bfloat16 [102400, 2048], P(('seq', 'exp')), may hold values from -4 to 4
Outputs:
- layer_out: bfloat16 [4, 1024, 2048], P('exp', 'seq')
- logprobs: float32 [16, 102400], P(None, ('seq', 'exp'))
Inputs may be any that keep to these rules, and one draw needn't show every extreme that they name: `routes`: in the rows of one device no expert is named by more than 56 rows; in some devices one expert is named by exactly 56 rows. `lengths`: each row sums to 1024; its largest entry is 512.
All inputs are finite; a program needn't handle non-finite values.
Results may differ from a plain program's by a relative error of at most 0.0095.
The roundings to bfloat16 on the way count: a program that leaves them out, or rounds other values in their place, can miss the bound.
Values may be sent and summed in bfloat16 or wider, within the bound.
No kernel may reach another device: no remote copies, remote signals or barrier semaphores. Data moves between devices by JAX's collectives and lax.ppermute only.
A program may use at most 128 MiB of HBM per device.

v0:
```python
import jax
import jax.numpy as jnp
from jax import lax
from jax.sharding import PartitionSpec as P

epsilon = 1e-06


def joined(value, axis, join):
    pieces = jax.tree.map(lambda part: lax.all_gather(part, axis), value)
    head = jax.tree.map(lambda part: part[0], pieces)
    tail = jax.tree.map(lambda part: part[1:], pieces)
    subtotal, _ = lax.scan(lambda subtotal, piece: (join(subtotal, piece), None), head, tail)
    return subtotal


def rms_scale(values, gain):
    widened = values.astype(jnp.float32)
    inverse = lax.rsqrt(jnp.mean(widened * widened, axis=-1, keepdims=True) + epsilon)
    return widened * inverse * gain


def segment_layout(prompt_lengths, count):
    ends = jnp.cumsum(prompt_lengths)
    starts = ends - prompt_lengths
    places = jnp.arange(count, dtype=jnp.int32)
    member = ((places[:, None] >= starts[None, :]) & (places[:, None] < ends[None, :])).astype(
        jnp.int32
    )
    numbers = jnp.arange(prompt_lengths.shape[0], dtype=jnp.int32)
    segment = jnp.sum(member * numbers[None, :], axis=1)
    offset = places - jnp.sum(member * starts[None, :], axis=1)
    return (segment, offset)


def rotary(values, positions):
    half_size = values.shape[-1] // 2
    freqs = 10000.0 ** (-2.0 * jnp.arange(half_size, dtype=jnp.float32) / values.shape[-1])
    angles = positions.astype(jnp.float32)[:, None] * freqs[None, :]
    cosine = jnp.cos(angles)[:, None, :]
    sine = jnp.sin(angles)[:, None, :]
    first_half = values[..., :half_size]
    second_half = values[..., half_size:]
    return jnp.concatenate(
        [first_half * cosine - second_half * sine, second_half * cosine + first_half * sine],
        axis=-1,
    )


def pair_swap(value):
    count = lax.axis_size("exp")
    return lax.ppermute(value, "exp", [(i, i ^ 1) for i in range(count)])


def merge_softmax(earlier, later):
    highest = jnp.maximum(earlier[0], later[0])
    return (
        highest,
        earlier[1] * jnp.exp(earlier[0] - highest) + later[1] * jnp.exp(later[0] - highest),
    )


def per_device(
    hidden,
    lengths,
    attn_gain,
    w_qkv,
    w_out,
    moe_gain,
    router,
    routes,
    w_gate_up,
    w_down,
    final_gain,
    lm_head,
):
    seq_count = lax.axis_size("seq")
    group_count = lax.axis_size("exp")
    device_count = seq_count * group_count
    token_rows = hidden[0]
    tok_rows = token_rows.shape[0]
    model_width = token_rows.shape[1]
    group_tokens = tok_rows * seq_count
    head_count = w_qkv.shape[2]
    head_size = w_qkv.shape[3]
    scale_factor = head_size ** (-0.5)
    prompt_lengths = lengths[0]
    segment, offset = segment_layout(prompt_lengths, group_tokens)
    normed = rms_scale(token_rows, attn_gain).astype(jnp.bfloat16)
    qkv_weight = w_qkv.reshape(model_width, 3 * head_count * head_size)
    qkv = jnp.dot(
        lax.all_gather(normed, "seq", axis=0, tiled=True),
        qkv_weight,
        preferred_element_type=jnp.float32,
    ).reshape(group_tokens, 3, head_count, head_size)
    query = rotary(qkv[:, 0], offset).astype(jnp.bfloat16)
    keys = rotary(qkv[:, 1], offset).astype(jnp.bfloat16)
    values = qkv[:, 2].astype(jnp.bfloat16)
    block_rows = min(512, group_tokens)
    key_places = jnp.arange(group_tokens, dtype=jnp.int32)

    def one_block(block_index):
        first_row = block_index * block_rows
        block_query = lax.dynamic_slice_in_dim(query, first_row, block_rows, 0)
        block_segment = lax.dynamic_slice_in_dim(segment, first_row, block_rows, 0)
        query_places = first_row + jnp.arange(block_rows, dtype=jnp.int32)
        scores = (
            jnp.einsum("qhd,khd->hqk", block_query, keys, preferred_element_type=jnp.float32)
            * scale_factor
        )
        allowed = (block_segment[:, None] == segment[None, :]) & (
            key_places[None, :] <= query_places[:, None]
        )
        scores = jnp.where(allowed[None], scores, -1e30)
        highest = jnp.max(scores, axis=2, keepdims=True)
        weights = jnp.exp(scores - highest)
        probs = (weights / jnp.sum(weights, axis=2, keepdims=True)).astype(jnp.bfloat16)
        return jnp.einsum("hqk,khd->qhd", probs, values, preferred_element_type=jnp.float32).astype(
            jnp.bfloat16
        )

    blocks = lax.map(one_block, jnp.arange(group_tokens // block_rows, dtype=jnp.int32))
    heads_flat = blocks.reshape(group_tokens, head_count * head_size)
    regrouped = lax.all_to_all(heads_flat, "seq", split_axis=0, concat_axis=1, tiled=True)
    core = lax.axis_index("exp") % 2
    half_size = head_size // 2
    own_half = lax.dynamic_slice_in_dim(w_out, core * half_size, half_size, axis=1)
    own_weight = lax.all_gather(own_half, "seq", axis=0, tiled=True)
    other_weight = pair_swap(own_weight)
    regrouped = regrouped.reshape(tok_rows, -1, head_size)
    own_heads = lax.dynamic_slice_in_dim(regrouped, core * half_size, half_size, axis=2)
    other_heads = lax.dynamic_slice_in_dim(regrouped, (1 - core) * half_size, half_size, axis=2)
    mixed = jnp.einsum(
        "thd,hdo->to", own_heads, own_weight, preferred_element_type=jnp.float32
    ) + jnp.einsum("thd,hdo->to", other_heads, other_weight, preferred_element_type=jnp.float32)
    middle = (token_rows.astype(jnp.float32) + mixed).astype(jnp.bfloat16)
    expert_in = rms_scale(middle, moe_gain).astype(jnp.bfloat16)
    logits = jnp.dot(expert_in, router, preferred_element_type=jnp.float32)
    expert_count = router.shape[1]
    token_routes = routes[0]
    top_count = token_routes.shape[1]
    expert_ids = jnp.arange(expert_count, dtype=jnp.int32)
    chosen_mask = token_routes[:, :, None] == expert_ids[None, None, :]
    chosen = jnp.sum(jnp.where(chosen_mask, logits[:, None, :], 0.0), axis=2)
    gates = jax.nn.softmax(chosen, axis=-1)
    capacity = max(2, tok_rows * top_count * 7 // (6 * expert_count))
    flat_mask = chosen_mask.reshape(tok_rows * top_count, expert_count).astype(jnp.int32)
    earlier_count = jnp.cumsum(flat_mask, axis=0) - flat_mask
    slot_index = jnp.sum(earlier_count * flat_mask, axis=1)
    target = (token_routes.reshape(-1) * capacity + slot_index).reshape(tok_rows, top_count)
    slot_total = expert_count * capacity
    placed = target[:, :, None] == jnp.arange(slot_total, dtype=jnp.int32)[None, None, :]
    dispatch_table = jnp.any(placed, axis=1).astype(jnp.bfloat16)
    slot_weights = jnp.sum(jnp.where(placed, gates[:, :, None], 0.0), axis=1)
    packed = lax.dot_general(
        dispatch_table, expert_in, (((0,), (0,)), ((), ())), preferred_element_type=jnp.float32
    ).astype(jnp.bfloat16)
    shares = device_count // expert_count
    assert capacity % shares == 0
    outgoing = packed.reshape(device_count, capacity // shares, model_width)
    gate_up = w_gate_up[0]
    down_weight = w_down[0]
    other_gate_up = pair_swap(gate_up)
    other_down = pair_swap(down_weight)
    arrived = lax.all_to_all(outgoing, ("seq", "exp"), split_axis=0, concat_axis=0, tiled=True)
    arrived_shape = arrived.shape
    flat_rows = arrived.reshape(-1, model_width)

    def share_part(pair, down):
        both = jnp.einsum("rd,gfd->rgf", flat_rows, pair, preferred_element_type=jnp.float32)
        act = (jax.nn.silu(both[:, 0]) * both[:, 1]).astype(jnp.bfloat16)
        part = jnp.dot(act, down, preferred_element_type=jnp.float32).astype(jnp.bfloat16)
        return part.astype(jnp.float32)

    part_sum = share_part(gate_up, down_weight) + share_part(other_gate_up, other_down)
    returned = lax.all_to_all(
        part_sum.astype(jnp.bfloat16).reshape(arrived_shape),
        ("seq", "exp"),
        split_axis=0,
        concat_axis=0,
        tiled=True,
    )
    summed = returned.reshape(slot_total, model_width).astype(jnp.float32)
    routed = jnp.dot(
        slot_weights, summed, precision=lax.Precision.HIGHEST, preferred_element_type=jnp.float32
    )
    layer_rows = (middle.astype(jnp.float32) + routed).astype(jnp.bfloat16)
    prompt_count = prompt_lengths.shape[0]
    last_places = jnp.cumsum(prompt_lengths) - 1
    here_places = lax.axis_index("seq") * tok_rows + jnp.arange(tok_rows, dtype=jnp.int32)
    select_table = (last_places[:, None] == here_places[None, :]).astype(jnp.bfloat16)
    picked = jnp.dot(select_table, layer_rows, preferred_element_type=jnp.float32)
    board = jnp.zeros((group_count * prompt_count, model_width), jnp.bfloat16)
    board = lax.dynamic_update_slice_in_dim(
        board, picked.astype(jnp.bfloat16), lax.axis_index("exp") * prompt_count, 0
    )
    last_rows = lax.psum(board, ("seq", "exp")).astype(jnp.float32)
    final = rms_scale(last_rows, final_gain).astype(jnp.bfloat16)
    vocab_scores = lax.dot_general(
        final, lm_head, (((1,), (1,)), ((), ())), preferred_element_type=jnp.float32
    )
    local_peak = jnp.max(vocab_scores, axis=1)
    local_total = jnp.sum(jnp.exp(vocab_scores - local_peak[:, None]), axis=1)
    global_peak, global_total = joined((local_peak, local_total), ("seq", "exp"), merge_softmax)
    logprobs = vocab_scores - (global_peak + jnp.log(global_total))[:, None]
    return (layer_rows[None], logprobs)


def solution(mesh):
    return jax.shard_map(
        per_device,
        mesh=mesh,
        in_specs=(
            P("exp", "seq", None),
            P("exp", None),
            P(),
            P(None, None, "seq", None),
            P("seq", None, None),
            P(),
            P(),
            P("exp", "seq", None),
            P(("seq", "exp"), None, None, None),
            P(("seq", "exp"), None, None),
            P(),
            P(("seq", "exp"), None),
        ),
        out_specs=(P("exp", "seq", None), P(None, ("seq", "exp"))),
        check_vma=False,
    )
```

profile of v0, /device:TPU:0, one launch (start us, length us, event | category | flops | bytes accessed | tf_op | source)
XLA Modules:
  0.0 637.5 jit_solution(17529622819611426284)
XLA Ops:
  7.2 1.3 fusion.48
  8.6 2.1 fusion.50
  10.7 0.8 constant_dynamic-slice_fusion.2
  11.8 8.0 %reshape.269 = bf16[2048,768]{1,0:T(8,128)(2,1)} reshape(bf16[2048,3,2,128]{3,2,1,0:T(2,128)(2,1)} %param.19) | data formatting | bytes 6291456 | tf_op jit(solution)/shard_map/reshape | solution.py:90
  19.8 4.8 copy.43
  24.7 1.0 multiply_cosine_fusion
  25.7 61.2 %all-gather.5.cloned.1.call-done = bf16[1024,2048]{1,0:T(8,128)(2,1)} async-done(((bf16[128,2048]{1,0:T(8,128)(2,1)}), bf16[1024,2048]{1,0:T(8,128)(2,1)}) %all-gather.5.cloned.1.call-update) | async-done | bytes 4194320 | tf_op jit(solution)/shard_map/all_gather | solution.py:92
  86.9 6.2 fusion.31
  93.6 1.2 copy-done.4
  95.2 1.4 fusion.51
  96.8 64.4 %all-gather.7.cloned.1.call-done = bf16[16,64,2048]{2,1,0:T(8,128)(2,1)} async-done(((bf16[2,64,2048]{2,1,0:T(8,128)(2,1)}), bf16[16,64,2048]{2,1,0:T(8,128)(2,1)}) %all-gather.7.cloned.1.call-update) | async-done | bytes 4194320 | tf_op jit(solution)/shard_map/all_gather | solution.py:128
  161.3 17.8 %while.24 = (s32[]{:T(128)}, bf16[2,512,2,128]{3,2,1,0:T(2,128)(2,1)S(1)}, s32[2]{0:T(128)S(1)}, s32[1024]{0:T(1024)S(1)}, bf16[1024,2,128]{0,2,1:T(8,128)(2,1)S...) while((s32[]{:T(128)}, ...), condition=%wide.region_7.8_spmd.clone, body=%wide.region_4.7_spmd.clone.sunk | while | flops 544867840 | bytes 11557047 | solution.py:122
  161.3 0.6 dynamic_slice.72
  162.6 0.6 fusion.116
  163.2 3.7 fusion.117
  166.9 2.9 fusion.118
  170.2 0.6 dynamic_slice.72
  171.5 0.6 fusion.116
  172.1 3.7 fusion.117
  175.8 2.9 fusion.118
  179.1 1.1 all_to_all.18
  180.2 3.7 all-to-all-start
  184.3 1.7 reduce-window.11
  186.7 0.5 fusion.33
  187.1 12.0 %all-to-all-done = bf16[8,128,256]{2,1,0:T(8,128)(2,1)S(1)} async-done(((bf16[8,128,256]{2,1,0:T(8,128)(2,1)}), bf16[8,128,256]{2,1,0:T(8,128)(2,1)S(1)}, u32[]{:S(2)}, u32[]{:S(2)}) %all-to-all-start) | async-done | bytes 524320 | tf_op jit(solution)/shard_map/all_to_all | solution.py:124
  199.4 2.9 convolution_bitcast_fusion.1
  202.4 3.1 multiply_reduce_fusion
  205.5 3.0 convolution_convert_fusion
  208.5 5.8 reshape.272
  214.3 3.7 all-to-all-start.1
  218.6 93.3 %all-to-all-done.1 = bf16[32,28,2048]{2,1,0:T(8,128)(2,1)} async-done(((bf16[32,28,2048]{2,1,0:T(8,128)(2,1)}), bf16[32,28,2048]{2,1,0:T(8,128)(2,1)}, u32[]{:S(2)}, u32[]{:S(2)}) %all-to-all-start.1) | async-done | bytes 3670048 | tf_op jit(solution)/shard_map/all_to_all | solution.py:165
  311.9 5.9 reshape.292
  317.8 9.4 %fusion.76 = f32[896,2,704]{0,2,1:T(8,128)S(1)} fusion(bf16[896,2048,1]{1,0,2:T(8,128)(2,1)} %reshape.292, bf16[1,2,704,2048]{3,2,1,0:T(8,128)(2,1)} %param.24), kind=kOutput, calls=%fused_computation.127 | convolution fusion | flops 5167382528 | bytes 14483456 | tf_op jit(solution)/shard_map/rd,gfd->rgf/dot_general | solution.py:170
  327.3 3.4 fusion.44
  330.7 8.4 %fusion.88 = f32[896,2,704]{0,2,1:T(8,128)S(1)} fusion(bf16[896,2048,1]{1,0,2:T(8,128)(2,1)S(1)} %copy-done.3, bf16[2,704,2048]{2,1,0:T(8,128)(2,1)} %collective-permute-done.1), kind=kOutput, calls=%fused_computation.134 | convolution fusion | flops 5167382528 | bytes 14483456 | tf_op jit(solution)/shard_map/rd,gfd->rgf/dot_general | solution.py:170
  339.2 6.9 %add_convert_fusion = bf16[896,2048]{1,0:T(8,128)(2,1)} fusion(bf16[896,2048]{1,0:T(8,128)(2,1)S(1)} %fusion.44, bf16[704,2048]{1,0:T(8,128)(2,1)} %collective-permute-done.2, f32[896,2,704]{0,2,1:T(8,128)S(1)} %fusion.88), kind=kOutput, calls=%fused_computation.31 | convolution fusion | flops 2596651008 | bytes 15269888 | tf_op jit(solution)/shard_map/dot_general | solution.py:172
  346.0 5.8 reshape.274
  351.9 4.1 all-to-all-start.2
  357.1 92.8 %all-to-all-done.2 = bf16[32,28,2048]{2,1,0:T(8,128)(2,1)} async-done(((bf16[32,28,2048]{2,1,0:T(8,128)(2,1)}), bf16[32,28,2048]{2,1,0:T(8,128)(2,1)}, u32[]{:S(2)}, u32[]{:S(2)}) %all-to-all-start.2) | async-done | bytes 3670048 | tf_op jit(solution)/shard_map/all_to_all | solution.py:176
  449.8 5.8 reshape.275
  455.7 3.9 fusion.40
  459.8 0.6 copy-done.6
  460.5 117.0 %all-reduce.5.cloned.1.call-done = bf16[16,2048]{1,0:T(8,128)(2,1)} async-done(((bf16[16,2048]{1,0:T(8,128)(2,1)}), bf16[16,2048]{1,0:T(8,128)(2,1)}) %all-reduce.5.cloned.1.call-update) | async-done | bytes 65552 | tf_op jit(solution)/shard_map/psum | solution.py:197
  577.5 1.0 fusion.54
  578.5 8.5 %fusion.87 = (f32[16]{0:T(128)S(1)}, f32[16,3200]{1,0:T(8,128)S(1)}) fusion(bf16[3200,2048]{1,0:T(8,128)(2,1)} %param.27, bf16[16,2048]{1,0:T(8,128)(2,1)} %all-reduce.5.cloned.1.call-done, f32[2048]{0:T(1024)S(1)} %copy-done.10, f32[16]{0:T(128)S(1)} %add_rsqrt_fusion), kind=kOutput, calls=%fused_computation.133 | convolution fusion | flops 209897456 | bytes 13385856 | tf_op jit(solution)/shard_map/dot_general | solution.py:199
  587.7 40.8 %all-reduce.2 = (f32[512]{0:T(512)S(1)}, f32[512]{0:T(512)S(1)}) all-reduce(f32[512]{0:T(512)S(1)} %dynamic-update-slice, f32[512]{0:T(512)S(1)} %dynamic-update-slice.1), channel_id=2, replica_groups=mesh['seq'=8,'exp'=4] {'seq','exp'}, use_global_device_ids=true, to_apply=%add | all-reduce | flops 1024 | bytes 8192
  628.8 1.3 while.23
  630.2 0.8 broadcast_subtract_fusion
  (122 shorter events, 7.4 us)
Async XLA Ops:
  7.2 3.5 copy-start
  7.2 4.4 copy-start.12
  7.2 79.7 %all-gather.5.cloned.1.call-start = ((), (), s32[]{:S(2)}) async-start(), calls=%async_computation.3 | async-start | bytes 4718592 | tf_op jit(solution)/shard_map/all_gather | solution.py:92
  10.6 150.7 %all-gather.7.cloned.1.call-start = ((), (), s32[]{:S(2)}) async-start(), calls=%async_computation.4 | async-start | bytes 4718592 | tf_op jit(solution)/shard_map/all_gather | solution.py:128
  93.1 1.7 copy-start.4
  161.3 41.1 %collective-permute-start = (bf16[16,64,2048]{2,1,0:T(8,128)(2,1)}, bf16[16,64,2048]{2,1,0:T(8,128)(2,1)}, u32[]{:S(2)}, u32[]{:S(2)}) collective-permute-start(bf16[16,64,2048]{2,1,0:T(8,128)(2,1)} %all-gather.7.cloned.1.call-done), channel_id=1, source_target_pairs={{0,1},{1,0},{2,3},{3,2},{4,5},{5,4},{6,7},{7,6},{8,9},{9,8},{10,11... | collective-permute-start | bytes 12582920 | tf_op jit(solution)/shard_map/ppermute | solution.py:52
  161.3 22.6 %copy-start.9 = (s32[1,128,6]{1,0,2:T(1,128)S(1)}, s32[1,128,6]{1,0,2:T(1,128)}, u32[]{:S(2)}) copy-start(s32[1,128,6]{1,0,2:T(1,128)} %param.23) | copy-start | bytes 9220
  180.2 18.9 %all-to-all-start = ((bf16[8,128,256]{2,1,0:T(8,128)(2,1)}), bf16[8,128,256]{2,1,0:T(8,128)(2,1)S(1)}, u32[]{:S(2)}, u32[]{:S(2)}) async-start(bf16[8,128,256]{2,1,0:T(8,128)(2,1)} %all_to_all.18), calls=%async_computation | async-start | bytes 1048576 | tf_op jit(solution)/shard_map/all_to_all | solution.py:124
  184.2 18.2 %copy-start.2 = (bf16[1,128,2048]{2,1,0:T(8,128)(2,1)S(1)}, bf16[1,128,2048]{2,1,0:T(8,128)(2,1)}, u32[]{:S(2)}) copy-start(bf16[1,128,2048]{2,1,0:T(8,128)(2,1)} %param.16) | copy-start | bytes 1572868
  202.4 3.1 copy-start.8
  214.3 97.6 %all-to-all-start.1 = ((bf16[32,28,2048]{2,1,0:T(8,128)(2,1)}), bf16[32,28,2048]{2,1,0:T(8,128)(2,1)}, u32[]{:S(2)}, u32[]{:S(2)}) async-start(bf16[32,28,2048]{2,1,0:T(8,128)(2,1)} %reshape.272), calls=%async_computation.1 | async-start | bytes 8388608 | tf_op jit(solution)/shard_map/all_to_all | solution.py:165
  218.1 112.7 %collective-permute-start.1 = (bf16[2,704,2048]{2,1,0:T(8,128)(2,1)}, bf16[2,704,2048]{2,1,0:T(8,128)(2,1)}, u32[]{:S(2)}, u32[]{:S(2)}) collective-permute-start(bf16[2,704,2048]{2,1,0:T(8,128)(2,1)} %bitcast.143), channel_id=1, source_target_pairs={{0,1},{1,0},{2,3},{3,2},{4,5},{5,4},{6,7},{7,6},{8,9},{9,8},{10,11... | collective-permute-start | bytes 17301512 | tf_op jit(solution)/shard_map/ppermute | solution.py:52
  218.3 120.9 %collective-permute-start.2 = (bf16[704,2048]{1,0:T(8,128)(2,1)}, bf16[704,2048]{1,0:T(8,128)(2,1)}, u32[]{:S(2)}, u32[]{:S(2)}) collective-permute-start(bf16[704,2048]{1,0:T(8,128)(2,1)} %bitcast.144), channel_id=1, source_target_pairs={{0,1},{1,0},{2,3},{3,2},{4,5},{5,4},{6,7},{7,6},{8,9},{9,8},{10,11... | collective-permute-start | bytes 8650760 | tf_op jit(solution)/shard_map/ppermute | solution.py:52
  317.8 9.4 %copy-start.11 = (bf16[1,704,2048]{2,1,0:T(8,128)(2,1)S(1)}, bf16[1,704,2048]{2,1,0:T(8,128)(2,1)}, u32[]{:S(2)}) copy-start(bf16[1,704,2048]{2,1,0:T(8,128)(2,1)} %param.25) | copy-start | bytes 8650756
  327.3 3.4 copy-start.3
  351.9 4.4 copy-start.7
  351.9 98.0 %all-to-all-start.2 = ((bf16[32,28,2048]{2,1,0:T(8,128)(2,1)}), bf16[32,28,2048]{2,1,0:T(8,128)(2,1)}, u32[]{:S(2)}, u32[]{:S(2)}) async-start(bf16[32,28,2048]{2,1,0:T(8,128)(2,1)} %reshape.274), calls=%async_computation.2 | async-start | bytes 8388608 | tf_op jit(solution)/shard_map/all_to_all | solution.py:176
  356.0 221.6 %all-reduce.5.cloned.1.call-start = ((), (), s32[]{:S(2)}) async-start(), calls=%async_computation.5 | async-start | bytes 131072 | tf_op jit(solution)/shard_map/psum | solution.py:197
  455.7 122.8 %copy-start.10 = (f32[2048]{0:T(1024)S(1)}, f32[2048]{0:T(1024)}, u32[]{:S(2)}) copy-start(f32[2048]{0:T(1024)} %param.26) | copy-start | bytes 24580
  459.6 127.4 %copy-start.5 = (bf16[128,2048]{1,0:T(8,128)(2,1)}, bf16[128,2048]{1,0:T(8,128)(2,1)S(1)}, u32[]{:S(2)}) copy-start(bf16[128,2048]{1,0:T(8,128)(2,1)S(1)} %fusion.40) | copy-start | bytes 1572868
  459.8 0.6 copy-start.6
  578.5 52.4 %copy-start.1 = (bf16[2,128,2048]{2,1,0:T(8,128)(2,1)S(1)}, bf16[2,128,2048]{2,1,0:T(8,128)(2,1)}, u32[]{:S(2)}) copy-start(bf16[2,128,2048]{2,1,0:T(8,128)(2,1)} %param.20) | copy-start | bytes 3145732
Sparse Core Ops, SparseCore 0:
  10.7 76.0 all-gather.4
  89.6 71.6 all-gather.6
  460.6 116.8 all-reduce.4
where the time goes:
time: 639 us; the launch traced here: 637 us
  waiting for transfers between devices  441 us (69%)
  matrix products  69.6 us (11%)
  local copies, waits for them, and re-layouts  45.9 us (7%)
  blocking collectives  40.8 us (6%)
  between operations  14.3 us (2%)
  starting transfers between devices  12.4 us (2%)
  other arithmetic  11.9 us (2%)
    psum x1, waiting for transfers between devices, per_device(): last_rows = lax.psum(board, ('seq', 'exp')).astype(jnp.float32)  117 us
    all_to_all x1, waiting for transfers between devices, per_device(): lax.all_to_all(outgoing, ('seq', 'exp'), split_axis=0, concat_axis=0, til...  93.3 us
    all_to_all x1, waiting for transfers between devices, per_device(): lax.all_to_all(part_sum.astype(jnp.bfloat16).reshape(arrived_shape), ('se...  92.8 us
    all_gather x1, waiting for transfers between devices, per_device(): own_weight = lax.all_gather(own_half, 'seq', axis=0, tiled=True)  64.4 us
    all_gather x1, waiting for transfers between devices, per_device(): lax.all_gather(normed, 'seq', axis=0, tiled=True)  61.2 us
    unnamed x1, blocking collectives  40.8 us
    dot_general x2, matrix products, share_part(): jnp.einsum('rd,gfd->rgf', flat_rows, pair, preferred_element_type=jnp.flo...  17.8 us
  transfers between devices with their start and end apart: 9, of which 6 were waited for; matrix products, arithmetic and copies ran while one was open for 12% of the time, Pallas kernels for 0%

commit v1 on v0

--- a/solution.py
+++ b/solution.py
@@ -4,6 +4,17 @@
 from jax.sharding import PartitionSpec as P
 
 epsilon = 1e-06
+
+
+def cut_along(x, dim, size):
+    before, after = (x.shape[:dim], x.shape[dim + 1 :])
+    return jnp.moveaxis(x.reshape(*before, size, -1, *after), dim, 0)
+
+
+def laid_out(blocks, dim):
+    blocks = jnp.moveaxis(blocks, 0, dim)
+    shape = blocks.shape
+    return blocks.reshape(*shape[:dim], shape[dim] * shape[dim + 1], *shape[dim + 2 :])
 
 
 def joined(value, axis, join):
@@ -121,7 +132,14 @@
 
     blocks = lax.map(one_block, jnp.arange(group_tokens // block_rows, dtype=jnp.int32))
     heads_flat = blocks.reshape(group_tokens, head_count * head_size)
-    regrouped = lax.all_to_all(heads_flat, "seq", split_axis=0, concat_axis=1, tiled=True)
+    devices, index = (lax.axis_size("seq"), lax.axis_index("seq"))
+    parts = cut_along(heads_flat, 0, devices)
+    outs = [parts[index]]
+    for step in range(1, devices):
+        sent = parts[index ^ step]
+        outs.append(lax.ppermute(sent, "seq", [(i_2, i_2 ^ step) for i_2 in range(devices)]))
+    parts = jnp.stack(outs)[index ^ jnp.arange(devices)]
+    regrouped = laid_out(parts, 1)
     core = lax.axis_index("exp") % 2
     half_size = head_size // 2
     own_half = lax.dynamic_slice_in_dim(w_out, core * half_size, half_size, axis=1)

time: 639 us -> 638 us (level)
  waiting for transfers between devices: 441 us -> 430 us
  starting transfers between devices: 12.4 us -> 21.7 us
    all_to_all x1 -> x0, waiting for transfers between devices: 12 us -> none  [per_device(): lax.all_to_all(heads_flat, 'seq', split_axis=0, concat_axis=1, tiled=True)]
    ppermute x0 -> x7, starting transfers between devices: none -> 11.3 us  [per_device(): lax.ppermute(sent, 'seq', [(i_2, i_2 ^ step) for i_2 in range(devices)])]
  transfers between devices with their start and end apart: 9 -> 15, of which waited for: 6 -> 7; matrix products, arithmetic and copies ran while one was open for 12% -> 12% of each run, Pallas kernels for 0% -> 0%
where the time goes in v1:
time: 638 us; the launch traced here: 636 us
  waiting for transfers between devices  430 us (67%)
  matrix products  69.6 us (11%)
  local copies, waits for them, and re-layouts  45.7 us (7%)
  blocking collectives  40.8 us (6%)
  starting transfers between devices  21.7 us (3%)
  between operations  14.4 us (2%)
  other arithmetic  11.9 us (2%)
    psum x1, waiting for transfers between devices, per_device(): last_rows = lax.psum(board, ('seq', 'exp')).astype(jnp.float32)  117 us
    all_to_all x1, waiting for transfers between devices, per_device(): lax.all_to_all(outgoing, ('seq', 'exp'), split_axis=0, concat_axis=0, til...  93.3 us
    all_to_all x1, waiting for transfers between devices, per_device(): lax.all_to_all(part_sum.astype(jnp.bfloat16).reshape(arrived_shape), ('se...  93 us
    all_gather x1, waiting for transfers between devices, per_device(): own_weight = lax.all_gather(own_half, 'seq', axis=0, tiled=True)  64.4 us
    all_gather x1, waiting for transfers between devices, per_device(): lax.all_gather(normed, 'seq', axis=0, tiled=True)  58 us
    unnamed x1, blocking collectives  40.8 us
    dot_general x2, matrix products, share_part(): jnp.einsum('rd,gfd->rgf', flat_rows, pair, preferred_element_type=jnp.flo...  17.8 us
  transfers between devices with their start and end apart: 15, of which 7 were waited for; matrix products, arithmetic and copies ran while one was open for 12% of the time, Pallas kernels for 0%

profile of v1, /device:TPU:0, one launch (start us, length us, event | category | flops | bytes accessed | tf_op | source)
XLA Modules:
  0.0 636.2 jit_solution(1930093998321858173)
XLA Ops:
  7.2 1.3 fusion.48
  8.6 2.1 fusion.50
  10.7 0.8 constant_dynamic-slice_fusion.2
  12.2 8.0 %reshape.276 = bf16[2048,768]{1,0:T(8,128)(2,1)} reshape(bf16[2048,3,2,128]{3,2,1,0:T(2,128)(2,1)} %param.19) | data formatting | bytes 6291456 | tf_op jit(solution)/shard_map/reshape | solution.py:101
  20.3 4.7 copy.43
  25.0 1.7 reduce-window.11
  27.9 1.0 multiply_cosine_fusion
  28.9 58.0 %all-gather.5.cloned.1.call-done = bf16[1024,2048]{1,0:T(8,128)(2,1)} async-done(((bf16[128,2048]{1,0:T(8,128)(2,1)}), bf16[1024,2048]{1,0:T(8,128)(2,1)}) %all-gather.5.cloned.1.call-update) | async-done | bytes 4194320 | tf_op jit(solution)/shard_map/all_gather | solution.py:103
  86.9 6.2 fusion.31
  93.6 1.2 copy-done.4
  95.2 1.4 fusion.51
  96.9 64.4 %all-gather.7.cloned.1.call-done = bf16[16,64,2048]{2,1,0:T(8,128)(2,1)} async-done(((bf16[2,64,2048]{2,1,0:T(8,128)(2,1)}), bf16[16,64,2048]{2,1,0:T(8,128)(2,1)}) %all-gather.7.cloned.1.call-update) | async-done | bytes 4194320 | tf_op jit(solution)/shard_map/all_gather | solution.py:146
  161.3 18.0 %while.24 = (s32[]{:T(128)}, bf16[2,512,2,128]{3,2,1,0:T(2,128)(2,1)S(1)}, s32[2]{0:T(128)S(1)}, s32[1024]{0:T(1024)S(1)}, bf16[1024,2,128]{0,2,1:T(8,128)(2,1)S...) while((s32[]{:T(128)}, ...), condition=%wide.region_7.8_spmd.clone, body=%wide.region_4.7_spmd.clone.sunk | while | flops 544867840 | bytes 11557047 | solution.py:133
  163.2 3.7 fusion.118
  166.9 2.9 fusion.119
  172.1 3.7 fusion.118
  175.9 2.9 fusion.119
  180.3 0.8 collective-permute-start.1
  181.1 2.1 collective-permute-start.2
  183.3 1.6 collective-permute-start.3
  184.8 1.3 collective-permute-start.4
  186.2 1.6 collective-permute-start.5
  187.8 3.2 collective-permute-start.6
  191.1 2.4 collective-permute-done.3
  193.4 2.0 collective-permute-done.4
  196.3 2.9 convolution_bitcast_fusion.1
  199.3 3.1 multiply_reduce_fusion
  202.4 3.0 convolution_convert_fusion
  205.4 5.8 reshape.278
  211.2 5.6 all-to-all-start
  217.4 93.3 %all-to-all-done = bf16[32,28,2048]{2,1,0:T(8,128)(2,1)} async-done(((bf16[32,28,2048]{2,1,0:T(8,128)(2,1)}), bf16[32,28,2048]{2,1,0:T(8,128)(2,1)}, u32[]{:S(2)}, u32[]{:S(2)}) %all-to-all-start) | async-done | bytes 3670048 | tf_op jit(solution)/shard_map/all_to_all | solution.py:183
  310.7 5.9 reshape.306
  316.6 9.4 %fusion.77 = f32[896,2,704]{0,2,1:T(8,128)S(1)} fusion(bf16[896,2048,1]{1,0,2:T(8,128)(2,1)} %reshape.306, bf16[1,2,704,2048]{3,2,1,0:T(8,128)(2,1)} %param.24), kind=kOutput, calls=%fused_computation.146 | convolution fusion | flops 5167382528 | bytes 14483456 | tf_op jit(solution)/shard_map/rd,gfd->rgf/dot_general | solution.py:188
  326.1 3.4 fusion.44
  329.5 8.4 %fusion.89 = f32[896,2,704]{0,2,1:T(8,128)S(1)} fusion(bf16[896,2048,1]{1,0,2:T(8,128)(2,1)S(1)} %copy-done.3, bf16[2,704,2048]{2,1,0:T(8,128)(2,1)} %collective-permute-done.8), kind=kOutput, calls=%fused_computation.153 | convolution fusion | flops 5167382528 | bytes 14483456 | tf_op jit(solution)/shard_map/rd,gfd->rgf/dot_general | solution.py:188
  337.9 6.9 %add_convert_fusion = bf16[896,2048]{1,0:T(8,128)(2,1)} fusion(bf16[896,2048]{1,0:T(8,128)(2,1)S(1)} %fusion.44, bf16[704,2048]{1,0:T(8,128)(2,1)} %collective-permute-done.9, f32[896,2,704]{0,2,1:T(8,128)S(1)} %fusion.89), kind=kOutput, calls=%fused_computation.32 | convolution fusion | flops 2596651008 | bytes 15269888 | tf_op jit(solution)/shard_map/dot_general | solution.py:190
  344.8 5.8 reshape.280
  350.6 4.1 all-to-all-start.1
  355.6 93.0 %all-to-all-done.1 = bf16[32,28,2048]{2,1,0:T(8,128)(2,1)} async-done(((bf16[32,28,2048]{2,1,0:T(8,128)(2,1)}), bf16[32,28,2048]{2,1,0:T(8,128)(2,1)}, u32[]{:S(2)}, u32[]{:S(2)}) %all-to-all-start.1) | async-done | bytes 3670048 | tf_op jit(solution)/shard_map/all_to_all | solution.py:194
  448.6 5.8 reshape.281
  454.4 3.9 fusion.40
  458.6 0.6 copy-done.6
  459.3 117.0 %all-reduce.5.cloned.1.call-done = bf16[16,2048]{1,0:T(8,128)(2,1)} async-done(((bf16[16,2048]{1,0:T(8,128)(2,1)}), bf16[16,2048]{1,0:T(8,128)(2,1)}) %all-reduce.5.cloned.1.call-update) | async-done | bytes 65552 | tf_op jit(solution)/shard_map/psum | solution.py:215
  576.3 1.0 fusion.54
  577.3 8.5 %fusion.88 = (f32[16]{0:T(128)S(1)}, f32[16,3200]{1,0:T(8,128)S(1)}) fusion(bf16[3200,2048]{1,0:T(8,128)(2,1)} %param.27, bf16[16,2048]{1,0:T(8,128)(2,1)} %all-reduce.5.cloned.1.call-done, f32[2048]{0:T(1024)S(1)} %copy-done.10, f32[16]{0:T(128)S(1)} %add_rsqrt_fusion), kind=kOutput, calls=%fused_computation.152 | convolution fusion | flops 209897456 | bytes 13385856 | tf_op jit(solution)/shard_map/dot_general | solution.py:217
  586.4 40.8 %all-reduce.2 = (f32[512]{0:T(512)S(1)}, f32[512]{0:T(512)S(1)}) all-reduce(f32[512]{0:T(512)S(1)} %dynamic-update-slice, f32[512]{0:T(512)S(1)} %dynamic-update-slice.1), channel_id=2, replica_groups=mesh['seq'=8,'exp'=4] {'seq','exp'}, use_global_device_ids=true, to_apply=%add | all-reduce | flops 1024 | bytes 8192
  627.6 1.3 while.23
  628.9 0.8 broadcast_subtract_fusion
  (145 shorter events, 11.6 us)
Async XLA Ops:
  7.2 3.5 copy-start
  7.2 4.5 copy-start.9
  7.2 4.8 copy-start.12
  7.2 79.7 %all-gather.5.cloned.1.call-start = ((), (), s32[]{:S(2)}) async-start(), calls=%async_computation.2 | async-start | bytes 4718592 | tf_op jit(solution)/shard_map/all_gather | solution.py:103
  10.6 150.7 %all-gather.7.cloned.1.call-start = ((), (), s32[]{:S(2)}) async-start(), calls=%async_computation.3 | async-start | bytes 4718592 | tf_op jit(solution)/shard_map/all_gather | solution.py:146
  93.1 1.7 copy-start.4
  161.3 38.0 %collective-permute-start.7 = (bf16[16,64,2048]{2,1,0:T(8,128)(2,1)}, bf16[16,64,2048]{2,1,0:T(8,128)(2,1)}, u32[]{:S(2)}, u32[]{:S(2)}) collective-permute-start(bf16[16,64,2048]{2,1,0:T(8,128)(2,1)} %all-gather.7.cloned.1.call-done), channel_id=1, source_target_pairs={{0,1},{1,0},{2,3},{3,2},{4,5},{5,4},{6,7},{7,6},{8,9},{9,8},{10,11... | collective-permute-start | bytes 12582920 | tf_op jit(solution)/shard_map/ppermute | solution.py:63
  179.7 5.1 collective-permute-start
  180.3 5.9 collective-permute-start.1
  181.1 6.7 %collective-permute-start.2 = (bf16[128,256]{1,0:T(8,128)(2,1)S(1)}, bf16[128,256]{1,0:T(8,128)(2,1)S(1)}, u32[]{:S(2)}, u32[]{:S(2)}) collective-permute-start(bf16[128,256]{1,0:T(8,128)(2,1)S(1)} %get-tuple-element.161), channel_id=1, source_target_pairs={{0,12},{4,8},{8,4},{12,0},{16,28},{20,24},{24,20},{28,16},{1,13},{... | collective-permute-start | bytes 196616 | tf_op jit(solution)/shard_map/ppermute | solution.py:140
  183.3 10.2 %collective-permute-start.3 = (bf16[128,256]{1,0:T(8,128)(2,1)S(1)}, bf16[128,256]{1,0:T(8,128)(2,1)S(1)}, u32[]{:S(2)}, u32[]{:S(2)}) collective-permute-start(bf16[128,256]{1,0:T(8,128)(2,1)S(1)} %get-tuple-element.160), channel_id=1, source_target_pairs={{0,16},{4,20},{8,24},{12,28},{16,0},{20,4},{24,8},{28,12},{1,17},{... | collective-permute-start | bytes 196616 | tf_op jit(solution)/shard_map/ppermute | solution.py:140
  184.8 10.6 %collective-permute-start.4 = (bf16[128,256]{1,0:T(8,128)(2,1)S(1)}, bf16[128,256]{1,0:T(8,128)(2,1)S(1)}, u32[]{:S(2)}, u32[]{:S(2)}) collective-permute-start(bf16[128,256]{1,0:T(8,128)(2,1)S(1)} %get-tuple-element.159), channel_id=1, source_target_pairs={{0,20},{4,16},{8,28},{12,24},{16,4},{20,0},{24,12},{28,8},{1,21},{... | collective-permute-start | bytes 196616 | tf_op jit(solution)/shard_map/ppermute | solution.py:140
  186.2 9.2 %collective-permute-start.5 = (bf16[128,256]{1,0:T(8,128)(2,1)S(1)}, bf16[128,256]{1,0:T(8,128)(2,1)S(1)}, u32[]{:S(2)}, u32[]{:S(2)}) collective-permute-start(bf16[128,256]{1,0:T(8,128)(2,1)S(1)} %get-tuple-element.158), channel_id=1, source_target_pairs={{0,24},{4,28},{8,16},{12,20},{16,8},{20,12},{24,0},{28,4},{1,25},{... | collective-permute-start | bytes 196616 | tf_op jit(solution)/shard_map/ppermute | solution.py:140
  187.8 7.6 %collective-permute-start.6 = (bf16[128,256]{1,0:T(8,128)(2,1)S(1)}, bf16[128,256]{1,0:T(8,128)(2,1)S(1)}, u32[]{:S(2)}, u32[]{:S(2)}) collective-permute-start(bf16[128,256]{1,0:T(8,128)(2,1)S(1)} %get-tuple-element.157), channel_id=1, source_target_pairs={{0,28},{4,24},{8,20},{12,16},{16,12},{20,8},{24,4},{28,0},{1,29},{... | collective-permute-start | bytes 196616 | tf_op jit(solution)/shard_map/ppermute | solution.py:140
  195.5 3.8 copy-start.2
  199.3 3.1 copy-start.8
  211.2 99.5 %all-to-all-start = ((bf16[32,28,2048]{2,1,0:T(8,128)(2,1)}), bf16[32,28,2048]{2,1,0:T(8,128)(2,1)}, u32[]{:S(2)}, u32[]{:S(2)}) async-start(bf16[32,28,2048]{2,1,0:T(8,128)(2,1)} %reshape.278), calls=%async_computation | async-start | bytes 8388608 | tf_op jit(solution)/shard_map/all_to_all | solution.py:183
  216.8 112.7 %collective-permute-start.8 = (bf16[2,704,2048]{2,1,0:T(8,128)(2,1)}, bf16[2,704,2048]{2,1,0:T(8,128)(2,1)}, u32[]{:S(2)}, u32[]{:S(2)}) collective-permute-start(bf16[2,704,2048]{2,1,0:T(8,128)(2,1)} %bitcast.173), channel_id=1, source_target_pairs={{0,1},{1,0},{2,3},{3,2},{4,5},{5,4},{6,7},{7,6},{8,9},{9,8},{10,11... | collective-permute-start | bytes 17301512 | tf_op jit(solution)/shard_map/ppermute | solution.py:63
  217.1 120.9 %collective-permute-start.9 = (bf16[704,2048]{1,0:T(8,128)(2,1)}, bf16[704,2048]{1,0:T(8,128)(2,1)}, u32[]{:S(2)}, u32[]{:S(2)}) collective-permute-start(bf16[704,2048]{1,0:T(8,128)(2,1)} %bitcast.174), channel_id=1, source_target_pairs={{0,1},{1,0},{2,3},{3,2},{4,5},{5,4},{6,7},{7,6},{8,9},{9,8},{10,11... | collective-permute-start | bytes 8650760 | tf_op jit(solution)/shard_map/ppermute | solution.py:63
  316.6 9.4 %copy-start.11 = (bf16[1,704,2048]{2,1,0:T(8,128)(2,1)S(1)}, bf16[1,704,2048]{2,1,0:T(8,128)(2,1)}, u32[]{:S(2)}) copy-start(bf16[1,704,2048]{2,1,0:T(8,128)(2,1)} %param.25) | copy-start | bytes 8650756
  326.1 3.4 copy-start.3
  350.6 4.2 copy-start.7
  350.6 98.0 %all-to-all-start.1 = ((bf16[32,28,2048]{2,1,0:T(8,128)(2,1)}), bf16[32,28,2048]{2,1,0:T(8,128)(2,1)}, u32[]{:S(2)}, u32[]{:S(2)}) async-start(bf16[32,28,2048]{2,1,0:T(8,128)(2,1)} %reshape.280), calls=%async_computation.1 | async-start | bytes 8388608 | tf_op jit(solution)/shard_map/all_to_all | solution.py:194
  354.7 221.6 %all-reduce.5.cloned.1.call-start = ((), (), s32[]{:S(2)}) async-start(), calls=%async_computation.4 | async-start | bytes 131072 | tf_op jit(solution)/shard_map/psum | solution.py:215
  454.4 122.8 %copy-start.10 = (f32[2048]{0:T(1024)S(1)}, f32[2048]{0:T(1024)}, u32[]{:S(2)}) copy-start(f32[2048]{0:T(1024)} %param.26) | copy-start | bytes 24580
  458.3 127.4 %copy-start.5 = (bf16[128,2048]{1,0:T(8,128)(2,1)}, bf16[128,2048]{1,0:T(8,128)(2,1)S(1)}, u32[]{:S(2)}) copy-start(bf16[128,2048]{1,0:T(8,128)(2,1)S(1)} %fusion.40) | copy-start | bytes 1572868
  458.6 0.6 copy-start.6
  577.3 52.4 %copy-start.1 = (bf16[2,128,2048]{2,1,0:T(8,128)(2,1)S(1)}, bf16[2,128,2048]{2,1,0:T(8,128)(2,1)}, u32[]{:S(2)}) copy-start(bf16[2,128,2048]{2,1,0:T(8,128)(2,1)} %param.20) | copy-start | bytes 3145732
Sparse Core Ops, SparseCore 0:
  10.8 76.0 all-gather.4
  89.6 71.6 all-gather.6
  459.4 116.8 all-reduce.4
